TPU v7x, 512 devices: a whole 4x4x16 slice. The times are simulated.
512 devices in a mesh: ctx: 64 (over z_lo, y, core), wa: 8 (over z_hi, x).
Axes of the slice: x: 4, y: 4, z: 16 (z_hi: 2, z_lo: 8; z = z_hi * 8 + z_lo), core: 2. Of those that a mesh axis runs over, the one named last changes fastest.
Arguments:
- q_nope: bfloat16 [512, 8192], P('ctx', 'wa'), may hold values from -6 to 6
- q_rope: bfloat16 [512, 4096], P('ctx', 'wa'), may hold values from -100 to 100
- w_uk: bfloat16 [64, 128, 512], P('wa'), may hold values from -0.25 to 0.25
- w_uv: bfloat16 [64, 512, 128], P('wa'), may hold values from -0.25 to 0.25
- cache: bfloat16 [32768, 576], P('ctx'), may hold values from -16 to 16
- cache_scale: float32 [32768], P('ctx'), may hold values from 0.5 to 2, as said below
- new_latent: bfloat16 [512, 576], P('ctx'), may hold values from -16 to 16
- cache_doc: int32 [512], P('ctx'), may hold values from 0 to 15
- new_lengths: int32 [16], replicated, may hold values from 1 to 128, 512 in all
Outputs:
- attn_out: bfloat16 [512, 8192], P('ctx', 'wa')
Inputs may be any that keep to these rules, and one draw needn't show every extreme that they name: `cache_scale`: each scale is 0.5, 1 or 2.
All inputs are finite; a program needn't handle non-finite values.
Results may differ from a plain program's by a relative error of at most 0.0064.
Values may be sent and summed in bfloat16 or wider, within the bound.
No kernel may reach another device: no remote copies, remote signals or barrier semaphores. Data moves between devices by JAX's collectives and lax.ppermute only.
A program may use at most 64 MiB of HBM per device.

v0:
```python
import jax
import jax.numpy as jnp
import numpy as np
from jax import lax
from jax.sharding import Mesh, PartitionSpec as P

CHIP_PARTS = ("cz", "cy")
CORE = "cc"


def doc_index(position, new_lengths):
    ends = jnp.cumsum(new_lengths)
    return jnp.sum((ends[None, :] <= position[:, None]).astype(jnp.int32), axis=1)


def absorb_rows(nope_rows, w_uk):
    row_count = nope_rows.shape[0]
    heads_dev, nope_dim, latent_dim = w_uk.shape
    shaped = nope_rows.reshape(row_count, heads_dev, nope_dim)
    absorbed = jnp.einsum("thn,hnl->thl", shaped, w_uk, preferred_element_type=jnp.float32)
    return absorbed.astype(jnp.bfloat16)


def chip_index():
    index = lax.axis_index(CHIP_PARTS[0])
    for name in CHIP_PARTS[1:]:
        index = index * lax.axis_size(name) + lax.axis_index(name)
    return index


def gather_rows(x):
    for name in reversed(CHIP_PARTS):
        x = lax.all_gather(x, name, axis=0, tiled=True)
    return x


def scatter_rows(x):
    for name in CHIP_PARTS:
        x = lax.psum_scatter(x, name, scatter_dimension=0, tiled=True)
    return x


def merge_stats(stats, heads_dev):
    for name in reversed(CHIP_PARTS):
        group = lax.all_gather(stats, name, axis=0, tiled=False)
        peak = jnp.max(group[:, :, :heads_dev], axis=0)
        shifted = jnp.where(jnp.isfinite(peak), peak, jnp.zeros_like(peak))
        scale = jnp.exp(group[:, :, :heads_dev] - shifted[None])
        total = jnp.sum(scale * group[:, :, heads_dev:], axis=0)
        stats = jnp.concatenate([peak, total], axis=1)
    return (stats[:, :heads_dev], stats[:, heads_dev:])


def swap_cores(x):
    return lax.ppermute(x, CORE, [(0, 1), (1, 0)])


def body(q_nope, q_rope, w_uk, w_uv, cache, cache_scale, new_latent, cache_doc, new_lengths):
    tok_rows = q_nope.shape[0]
    heads_dev, nope_dim, latent_dim = w_uk.shape
    value_dim = w_uv.shape[2]
    rope_dim = q_rope.shape[1] // heads_dev
    cores = lax.axis_size(CORE)
    chips = 1
    for name in CHIP_PARTS:
        chips = chips * lax.axis_size(name)
    q_rows = tok_rows * chips
    my_chip = chip_index()
    my_core = lax.axis_index(CORE)
    other_core = 1 - my_core
    score_scale = (nope_dim + rope_dim) ** (-0.5)
    dequant = (cache.astype(jnp.float32) * cache_scale[:, None]).astype(jnp.bfloat16)
    own_keys = jnp.concatenate([dequant, new_latent], axis=0)
    other_keys = swap_cores(own_keys)
    other_doc = swap_cores(cache_doc)
    own_q = jnp.concatenate([q_nope, q_rope], axis=1)
    all_q = gather_rows(own_q)
    nope_width = heads_dev * nope_dim
    all_lat = absorb_rows(all_q[:, :nope_width], w_uk)
    all_rope = all_q[:, nope_width:]
    query = jnp.concatenate([all_lat, all_rope.reshape(q_rows, heads_dev, rope_dim)], axis=2)
    cache_len = cache.shape[0]
    block_len = cache_len // cache_doc.shape[0]
    row = jnp.arange(q_rows, dtype=jnp.int32)
    query_pos = (row // tok_rows * cores + my_core) * tok_rows + row % tok_rows
    query_doc = doc_index(query_pos, new_lengths)

    def key_meta(core, docs):
        new_pos = (my_chip * cores + core) * tok_rows + jnp.arange(tok_rows, dtype=jnp.int32)
        key_doc = jnp.concatenate([jnp.repeat(docs, block_len), doc_index(new_pos, new_lengths)])
        key_pos = jnp.concatenate([jnp.full((cache_len,), -1, dtype=jnp.int32), new_pos])
        return (key_doc, key_pos)

    own_doc, own_pos = key_meta(my_core, cache_doc)
    far_doc, far_pos = key_meta(other_core, other_doc)
    key_rows = jnp.concatenate([own_keys, other_keys], axis=0)
    key_doc = jnp.concatenate([own_doc, far_doc])
    key_pos = jnp.concatenate([own_pos, far_pos])
    allowed = (query_doc[:, None] == key_doc[None, :]) & (key_pos[None, :] <= query_pos[:, None])
    score = (
        jnp.einsum("qhl,kl->qhk", query, key_rows, preferred_element_type=jnp.float32) * score_scale
    )
    masked = jnp.where(allowed[:, None, :], score, -jnp.inf)
    local_max = jnp.max(masked, axis=2)
    shift = jnp.where(jnp.isfinite(local_max), local_max, jnp.zeros_like(local_max))
    weight = jnp.exp(masked - shift[:, :, None])
    totals = jnp.sum(weight, axis=2)
    weight_low = weight.astype(jnp.bfloat16)
    part_lat = jnp.einsum(
        "qhk,kl->qhl", weight_low, key_rows[:, :latent_dim], preferred_element_type=jnp.float32
    ).astype(jnp.bfloat16)
    numerator = jnp.einsum("qhl,hlv->qhv", part_lat, w_uv, preferred_element_type=jnp.float32)
    row_max, row_total = merge_stats(jnp.concatenate([local_max, totals], axis=1), heads_dev)
    factor = jnp.exp(local_max - row_max)
    scaled = (numerator * factor[:, :, None]).reshape(q_rows, heads_dev * value_dim)
    own_numer = scatter_rows(scaled).reshape(tok_rows, heads_dev, value_dim)
    own_total = lax.dynamic_slice_in_dim(row_total, my_chip * tok_rows, tok_rows, axis=0)
    result = own_numer / own_total[:, :, None]
    return result.astype(jnp.bfloat16).reshape(tok_rows, heads_dev * value_dim)


def solution(mesh):
    ctx_shape = (8, 4, 2)
    grid = np.asarray(mesh.devices).reshape(ctx_shape + (mesh.shape["wa"],))
    fine = Mesh(grid, CHIP_PARTS + (CORE, "wa"))
    rows = CHIP_PARTS + (CORE,)
    placed = (
        P(rows, "wa"),
        P(rows, "wa"),
        P("wa", None, None),
        P("wa", None, None),
        P(rows, None),
        P(rows),
        P(rows, None),
        P(rows),
        P(),
    )
    return jax.shard_map(body, mesh=fine, in_specs=placed, out_specs=P(rows, "wa"), check_vma=False)
```

profile of v0, /device:TPU:2, one launch (start us, length us, event | category | flops | bytes accessed | tf_op | source)
XLA Modules:
  0.0 268.3 jit_solution(17568479425091766491)
XLA Ops:
  6.6 2.1 collective-permute-start
  8.6 0.9 copy.64
  9.5 1.2 multiply_convert_fusion
  10.8 1.1 copy.63
  12.0 2.4 collective-permute-start.1
  14.4 0.1 copy.57
  14.5 0.1 reduce
  14.7 12.4 %all_gather.18 = bf16[32,1536]{1,0:T(8,128)(2,1)S(1)} all-gather(bf16[8,1536]{1,0:T(8,128)(2,1)S(1)} %pad_maximum_fusion.1), channel_id=1, replica_groups=mesh['cz'=8,'cy'=4,'cc'=2,'wa'=8] {'cy'}, dimensions={0}, use_global_device_ids=true | all-gather | bytes 122880 | tf_op jit(solution)/shard_map/all_gather | solution.py:33
  27.2 51.2 %all_gather.19 = bf16[256,1536]{1,0:T(8,128)(2,1)S(1)} all-gather(bf16[32,1536]{1,0:T(8,128)(2,1)S(1)} %all_gather.18), channel_id=1, replica_groups=mesh['cz'=8,'cy'=4,'cc'=2,'wa'=8] {'cz'}, dimensions={0}, use_global_device_ids=true | all-gather | bytes 884736 | tf_op jit(solution)/shard_map/all_gather | solution.py:33
  78.4 0.2 copy.75
  78.6 0.1 convert_reduce_fusion
  78.7 2.1 convert_bitcast_fusion
  80.9 0.1 reshape.143
  81.0 0.1 copy.76
  81.2 0.3 copy.61
  81.5 0.1 concatenate.26
  81.6 0.2 convert_reduce_fusion.1
  81.9 0.1 concatenate.25
  82.0 0.7 compare_and_fusion
  82.8 1.4 copy.65
  84.2 2.1 concatenate.30
  86.3 6.2 %fusion = (f32[256,8]{0,1:T(8,128)S(1)}, f32[256,8,1040]{0,2,1:T(8,128)S(1)}) fusion(pred[256,1040]{0,1:T(8,128)(4,1)S(1)} %compare_and_fusion, bf16[1040,576]{0,1:T(8,128)(2,1)} %concatenate.30, bf16[256,8,64]{2,0,1:T(8,128)(2,1)S(1)} %copy.61, bf16[256,8,512]{2,0,1:T(8,128)(2,1)} %convert_bitcast_fusion), kind=kOutput, calls=%fused_computation.2 | convolution fusion | flops 2464774144 | bytes 12351488 | tf_op jit(solution)/shard_map/qhl,kl->qhk/dot_general | solution.py:101
  92.5 1.7 fusion.1
  94.3 1.5 copy-done.1
  95.8 11.9 %all-gather = f32[1024,16]{0,1:T(8,128)S(1)} all-gather(f32[256,16]{0,1:T(8,128)S(1)} %pad_maximum_fusion.2), channel_id=2, replica_groups=mesh['cz'=8,'cy'=4,'cc'=2,'wa'=8] {'cy'}, dimensions={0}, use_global_device_ids=true | all-gather | bytes 81920 | tf_op jit(solution)/shard_map/all_gather | solution.py:45
  107.8 46.6 %all-gather.1 = f32[2048,16]{0,1:T(8,128)S(1)} all-gather(f32[256,16]{0,1:T(8,128)S(1)} %pad_maximum_fusion.3), channel_id=3, replica_groups=mesh['cz'=8,'cy'=4,'cc'=2,'wa'=8] {'cz'}, dimensions={0}, use_global_device_ids=true | all-gather | bytes 147456 | tf_op jit(solution)/shard_map/all_gather | solution.py:45
  154.5 8.4 %fusion.24 = f32[256,8,128]{0,2,1:T(8,128)} fusion(bf16[8,512,128]{2,1,0:T(8,128)(2,1)} %param.12, f32[256,8,1040]{0,2,1:T(8,128)} %copy-done.1, f32[256,8]{0,1:T(8,128)S(1)} %is-finite_select_fusion.2, pred[256,1040]{0,1:T(8,128)(4,1)S(1)} %compare_and_fusion, bf16[1040,576]{0,1:T(8,128)(2,1)S(1)} %copy-done.4, f32[256,8]{0,1:T(8,128)S(1)} %get-tuple-element.8), kind=kOutput, calls=%fused_computation.18 | convolution fusion | flops 2459303936 | bytes 12079104 | tf_op jit(solution)/shard_map/qhl,hlv->qhv/dot_general | solution.py:112
  162.9 2.5 copy.69
  165.5 70.0 %reduce-scatter.3.cloned.1.call-done = f32[32,1024]{1,0:T(8,128)} async-done(((f32[256,1024]{1,0:T(8,128)}), f32[32,1024]{1,0:T(8,128)}) %reduce-scatter.3.cloned.1.call-update) | async-done | bytes 131088 | tf_op jit(solution)/shard_map/reduce_scatter | solution.py:39
  235.6 0.1 constant_dynamic-slice_fusion
  235.7 24.4 %reduce-scatter.5.cloned.1.call-done = f32[8,1024]{1,0:T(8,128)} async-done(((f32[32,1024]{1,0:T(8,128)}), f32[8,1024]{1,0:T(8,128)}) %reduce-scatter.5.cloned.1.call-update) | async-done | bytes 32784 | tf_op jit(solution)/shard_map/reduce_scatter | solution.py:39
  260.1 1.4 fusion.32
  (45 shorter events, 0.8 us)
Async XLA Ops:
  6.5 72.2 %copy-start = (bf16[8,128,512]{2,1,0:T(8,128)(2,1)S(1)}, bf16[8,128,512]{2,1,0:T(8,128)(2,1)}, u32[]{:S(2)}) copy-start(bf16[8,128,512]{2,1,0:T(8,128)(2,1)} %param.11) | copy-start | bytes 3145732
  6.5 7.9 %copy-start.7 = (s32[16]{0:T(128)S(1)}, s32[16]{0:T(128)}, u32[]{:S(2)}) copy-start(s32[16]{0:T(128)} %param.17) | copy-start | bytes 196
  6.5 8.1 %copy-start.6 = (bf16[8,512]{1,0:T(8,128)(2,1)S(1)}, bf16[8,512]{1,0:T(8,128)(2,1)}, u32[]{:S(2)}) copy-start(bf16[8,512]{1,0:T(8,128)(2,1)} %param.10) | copy-start | bytes 24580
  6.5 8.1 %copy-start.5 = (bf16[8,1024]{1,0:T(8,128)(2,1)S(1)}, bf16[8,1024]{1,0:T(8,128)(2,1)}, u32[]{:S(2)}) copy-start(bf16[8,1024]{1,0:T(8,128)(2,1)} %param.9) | copy-start | bytes 49156
  6.5 229.0 %reduce-scatter.3.cloned.1.call-start = ((), (), s32[]{:S(2)}) async-start(), calls=%async_computation.2 | async-start | bytes 1179648 | tf_op jit(solution)/shard_map/reduce_scatter | solution.py:39
  6.6 75.2 %collective-permute-start = (s32[8]{0:T(128)}, s32[8]{0:T(128)S(1)}, u32[]{:S(2)}, u32[]{:S(2)}) collective-permute-start(s32[8]{0:T(128)} %param.16), channel_id=1, source_target_pairs={{0,8},{8,0},{1,9},{9,1},{2,10},{10,2},{3,11},{11,3},{4,12},{12,4},... | collective-permute-start | bytes 104 | tf_op jit(solution)/shard_map/ppermute | solution.py:55
  9.5 5.2 %copy-start.2 = (bf16[8,576]{0,1:T(8,128)(2,1)}, bf16[8,576]{0,1:T(8,128)(2,1)S(1)}, u32[]{:S(2)}) copy-start(bf16[8,576]{0,1:T(8,128)(2,1)S(1)} %copy.64) | copy-start | bytes 27652
  12.0 70.8 %collective-permute-start.1 = (bf16[520,576]{1,0:T(8,128)(2,1)}, bf16[520,576]{1,0:T(8,128)(2,1)}, u32[]{:S(2)}, u32[]{:S(2)}) collective-permute-start(bf16[520,576]{1,0:T(8,128)(2,1)} %copy.63), channel_id=1, source_target_pairs={{0,8},{8,0},{1,9},{9,1},{2,10},{10,2},{3,11},{11,3},{4,12},{12,4},... | collective-permute-start | bytes 1797128 | tf_op jit(solution)/shard_map/ppermute | solution.py:55
  78.4 2.4 copy-start.8
  80.8 3.4 %copy-start.3 = (bf16[8,576]{0,1:T(8,128)(2,1)S(1)}, bf16[8,576]{0,1:T(8,128)(2,1)}, u32[]{:S(2)}) copy-start(bf16[8,576]{0,1:T(8,128)(2,1)} %copy-done.2) | copy-start | bytes 27652
  92.5 3.3 %copy-start.1 = (f32[256,8,1040]{0,2,1:T(8,128)}, f32[256,8,1040]{0,2,1:T(8,128)S(1)}, u32[]{:S(2)}) copy-start(f32[256,8,1040]{0,2,1:T(8,128)S(1)} %get-tuple-element.10) | copy-start | bytes 25559044
  92.5 62.0 %copy-start.4 = (bf16[1040,576]{0,1:T(8,128)(2,1)S(1)}, bf16[1040,576]{0,1:T(8,128)(2,1)}, u32[]{:S(2)}) copy-start(bf16[1040,576]{0,1:T(8,128)(2,1)} %concatenate.30) | copy-start | bytes 3594244
  165.5 94.6 %reduce-scatter.5.cloned.1.call-start = ((), (), s32[]{:S(2)}) async-start(), calls=%async_computation.3 | async-start | bytes 163840 | tf_op jit(solution)/shard_map/reduce_scatter | solution.py:39
Sparse Core Ops, SparseCore 0:
  165.6 69.9 reduce-scatter.2
  238.3 21.6 reduce-scatter.4
where the time goes:
time: 269 us; the launch traced here: 268 us
  blocking collectives  122 us (45%)
  waiting for transfers between devices  94.4 us (35%)
  matrix products  16.7 us (6%)
  between operations  13.7 us (5%)
  local copies, waits for them, and re-layouts  11.1 us (4%)
  other arithmetic  5.83 us (2%)
  starting transfers between devices  4.52 us (2%)
    reduce_scatter x2, waiting for transfers between devices, scatter_rows(): x = lax.psum_scatter(x, name, scatter_dimension=0, tiled=True)  94.4 us
    all_gather x2, blocking collectives, gather_rows(): x = lax.all_gather(x, name, axis=0, tiled=True)  63.7 us
    all_gather x2, blocking collectives, merge_stats(): group = lax.all_gather(stats, name, axis=0, tiled=False)  58.4 us
    dot_general x1, matrix products, body(): jnp.einsum('qhl,hlv->qhv', part_lat, w_uv, preferred_element_type=jnp.flo...  8.42 us
    dot_general x1, matrix products, body(): jnp.einsum('qhl,kl->qhk', query, key_rows, preferred_element_type=jnp.flo...  6.18 us
  transfers between devices with their start and end apart: 4, of which 2 were waited for; matrix products, arithmetic and copies ran while one was open for 3% of the time, Pallas kernels for 0%

commit v1 on v0

--- a/solution.py
+++ b/solution.py
@@ -30,7 +30,12 @@
 
 def gather_rows(x):
     for name in reversed(CHIP_PARTS):
-        x = lax.all_gather(x, name, axis=0, tiled=True)
+        x = jnp.concatenate(
+            lax.all_to_all(
+                jnp.stack(tuple((x for _ in range(lax.axis_size(name)))), 0), name, 0, 0
+            ),
+            0,
+        )
     return x
 
 

time: 269 us -> 248 us (0.922)
  blocking collectives: 122 us -> 68.4 us
  waiting for transfers between devices: 94.4 us -> 115 us
  starting transfers between devices: 4.52 us -> 17.1 us
  matrix products: 16.7 us -> 13.4 us
  local copies, waits for them, and re-layouts: 11.1 us -> 14.1 us
    all_gather x2 -> x0, blocking collectives: 63.7 us -> none  [gather_rows(): x = lax.all_gather(x, name, axis=0, tiled=True)]
    all_to_all x0 -> x1, waiting for transfers between devices: none -> 26.8 us  [gather_rows(): lax.all_to_all(jnp.stack(tuple((x for _ in range(lax.axis_size(name)))),...]
    all_to_all x0 -> x1, starting transfers between devices: none -> 12.7 us  [gather_rows(): lax.all_to_all(jnp.stack(tuple((x for _ in range(lax.axis_size(name)))),...]
    all_to_all x0 -> x1, blocking collectives: none -> 10.1 us  [gather_rows(): lax.all_to_all(jnp.stack(tuple((x for _ in range(lax.axis_size(name)))),...]
    reduce_scatter x2, waiting for transfers between devices: 94.4 us -> 88.2 us  [scatter_rows(): x = lax.psum_scatter(x, name, scatter_dimension=0, tiled=True)]
  transfers between devices with their start and end apart: 4 -> 5, of which waited for: 2 -> 3; matrix products, arithmetic and copies ran while one was open for 3% -> 3% of each run, Pallas kernels for 0% -> 0%
where the time goes in v1:
time: 248 us
  waiting for transfers between devices  115 us (46%)
  blocking collectives  68.4 us (28%)
  starting transfers between devices  17.1 us (7%)
  local copies, waits for them, and re-layouts  14.1 us (6%)
  between operations  13.7 us (6%)
  matrix products  13.4 us (5%)
  other arithmetic  6.2 us (2%)
    reduce_scatter x2, waiting for transfers between devices, scatter_rows(): x = lax.psum_scatter(x, name, scatter_dimension=0, tiled=True)  88.2 us
    all_gather x2, blocking collectives, merge_stats(): group = lax.all_gather(stats, name, axis=0, tiled=False)  58.3 us
    all_to_all x1, waiting for transfers between devices, gather_rows(): lax.all_to_all(jnp.stack(tuple((x for _ in range(lax.axis_size(name)))),...  26.8 us
    all_to_all x1, starting transfers between devices, gather_rows(): lax.all_to_all(jnp.stack(tuple((x for _ in range(lax.axis_size(name)))),...  12.7 us
    all_to_all x1, blocking collectives, gather_rows(): lax.all_to_all(jnp.stack(tuple((x for _ in range(lax.axis_size(name)))),...  10.1 us
    dot_general x1, matrix products, body(): jnp.einsum('qhl,hlv->qhv', part_lat, w_uv, preferred_element_type=jnp.flo...  8.41 us
  transfers between devices with their start and end apart: 5, of which 3 were waited for; matrix products, arithmetic and copies ran while one was open for 3% of the time, Pallas kernels for 0%

profile of v1, /device:TPU:2, one launch (start us, length us, event | category | flops | bytes accessed | tf_op | source)
XLA Modules:
  0.0 247.8 jit_solution(4422051015866214142)
XLA Ops:
  6.5 0.9 pad_maximum_fusion.1
  7.4 10.1 %all_to_all.10 = bf16[4,8,1536]{2,1,0:T(8,128)(2,1)S(1)} all-to-all(bf16[4,8,1536]{2,1,0:T(8,128)(2,1)S(1)} %stack.4), channel_id=1, replica_groups=mesh['cz'=8,'cy'=4,'cc'=2,'wa'=8] {'cy'}, dimensions={0} | all-to-all | bytes 196608 | tf_op jit(solution)/shard_map/all_to_all | solution.py:34
  17.5 1.0 stack.5
  18.5 12.7 %all-to-all-start.1 = ((bf16[8,32,1536]{2,1,0:T(8,128)(2,1)}), bf16[8,32,1536]{2,1,0:T(8,128)(2,1)S(1)}, u32[]{:S(2)}, u32[]{:S(2)}) async-start(bf16[8,32,1536]{2,1,0:T(8,128)(2,1)} %stack.5), calls=%async_computation.1 | async-start | bytes 1572864 | tf_op jit(solution)/shard_map/all_to_all | solution.py:34
  31.2 1.9 collective-permute-start
  33.1 0.2 copy.51
  33.3 0.1 multiply_convert_fusion
  33.5 1.1 copy.50
  34.6 2.4 collective-permute-start.1
  37.2 0.1 reduce
  37.3 0.1 convert_reduce_fusion
  37.6 0.2 convert_reduce_fusion.1
  38.1 1.4 compare_and_fusion
  39.5 1.4 copy.52
  40.9 2.0 concatenate.30
  43.0 26.8 %all-to-all-done.1 = bf16[8,32,1536]{2,1,0:T(8,128)(2,1)S(1)} async-done(((bf16[8,32,1536]{2,1,0:T(8,128)(2,1)}), bf16[8,32,1536]{2,1,0:T(8,128)(2,1)S(1)}, u32[]{:S(2)}, u32[]{:S(2)}) %all-to-all-start.1) | async-done | bytes 786464 | tf_op jit(solution)/shard_map/all_to_all | solution.py:34
  69.7 0.7 slice.31
  70.5 0.2 copy.45
  70.8 1.2 copy.47
  72.0 1.0 copy.48
  73.0 0.8 convert_bitcast_fusion
  73.8 0.3 copy-done.5
  74.0 4.3 %fusion = (f32[256,8]{0,1:T(8,128)S(1)}, f32[256,8,1040]{0,2,1:T(8,128)S(1)}) fusion(pred[256,1040]{0,1:T(8,128)(4,1)S(1)} %copy-done.3, bf16[1040,576]{0,1:T(8,128)(2,1)S(1)} %copy-done.2, bf16[256,8,64]{2,0,1:T(8,128)(2,1)S(1)} %copy-done.5, bf16[256,8,512]{2,0,1:T(8,128)(2,1)S(1)} %convert_bitcast_fusion), kind=kOutput, calls=%fused_computation.2 | convolution fusion | flops 2464774144 | bytes 12351488 | tf_op jit(solution)/shard_map/qhl,kl->qhk/dot_general | solution.py:106
  78.3 1.7 fusion.1
  80.1 1.5 copy-done.1
  81.6 11.9 %all-gather = f32[1024,16]{0,1:T(8,128)S(1)} all-gather(f32[256,16]{0,1:T(8,128)S(1)} %pad_maximum_fusion.2), channel_id=2, replica_groups=mesh['cz'=8,'cy'=4,'cc'=2,'wa'=8] {'cy'}, dimensions={0}, use_global_device_ids=true | all-gather | bytes 81920 | tf_op jit(solution)/shard_map/all_gather | solution.py:50
  93.6 46.5 %all-gather.1 = f32[2048,16]{0,1:T(8,128)S(1)} all-gather(f32[256,16]{0,1:T(8,128)S(1)} %pad_maximum_fusion.3), channel_id=3, replica_groups=mesh['cz'=8,'cy'=4,'cc'=2,'wa'=8] {'cz'}, dimensions={0}, use_global_device_ids=true | all-gather | bytes 147456 | tf_op jit(solution)/shard_map/all_gather | solution.py:50
  140.1 8.4 %fusion.24 = f32[256,8,128]{0,2,1:T(8,128)} fusion(bf16[8,512,128]{2,1,0:T(8,128)(2,1)} %param.12, f32[256,8,1040]{0,2,1:T(8,128)} %copy-done.1, f32[256,8]{0,1:T(8,128)S(1)} %is-finite_select_fusion.2, pred[256,1040]{0,1:T(8,128)(4,1)S(1)} %copy-done.3, bf16[1040,576]{0,1:T(8,128)(2,1)S(1)} %copy-done.2, f32[256,8]{0,1:T(8,128)S(1)} %get-tuple-element.8), kind=kOutput, calls=%fused_computation.18 | convolution fusion | flops 2459303936 | bytes 12079104 | tf_op jit(solution)/shard_map/qhl,hlv->qhv/dot_general | solution.py:117
  148.5 2.5 %copy.56 = f32[256,1024]{1,0:T(8,128)} copy(f32[256,1024]{0,1:T(8,128)} %bitcast.38) | data formatting | bytes 2097152 | tf_op jit(solution)/shard_map/reshape | solution.py:120
  151.1 63.6 %reduce-scatter.3.cloned.1.call-done = f32[32,1024]{1,0:T(8,128)} async-done(((f32[256,1024]{1,0:T(8,128)}), f32[32,1024]{1,0:T(8,128)}) %reduce-scatter.3.cloned.1.call-update) | async-done | bytes 131088 | tf_op jit(solution)/shard_map/reduce_scatter | solution.py:44
  214.9 24.6 %reduce-scatter.5.cloned.1.call-done = f32[8,1024]{1,0:T(8,128)} async-done(((f32[32,1024]{1,0:T(8,128)}), f32[8,1024]{1,0:T(8,128)}) %reduce-scatter.5.cloned.1.call-update) | async-done | bytes 32784 | tf_op jit(solution)/shard_map/reduce_scatter | solution.py:44
  239.5 1.4 fusion.32
  (50 shorter events, 1.2 us)
Async XLA Ops:
  6.5 66.5 %copy-start = (bf16[8,128,512]{2,1,0:T(8,128)(2,1)S(1)}, bf16[8,128,512]{2,1,0:T(8,128)(2,1)}, u32[]{:S(2)}) copy-start(bf16[8,128,512]{2,1,0:T(8,128)(2,1)} %param.11) | copy-start | bytes 3145732
  6.5 24.7 %copy-start.9 = (s32[8]{0:T(128)S(1)}, s32[8]{0:T(128)}, u32[]{:S(2)}) copy-start(s32[8]{0:T(128)} %param.16) | copy-start | bytes 100
  6.5 26.6 %copy-start.6 = (bf16[8,576]{1,0:T(8,128)(2,1)S(1)}, bf16[8,576]{1,0:T(8,128)(2,1)}, u32[]{:S(2)}) copy-start(bf16[8,576]{1,0:T(8,128)(2,1)} %param.15) | copy-start | bytes 27652
  6.5 26.8 %copy-start.7 = (f32[512]{0:T(512)S(1)}, f32[512]{0:T(512)}, u32[]{:S(2)}) copy-start(f32[512]{0:T(512)} %param.14) | copy-start | bytes 6148
  6.5 26.8 %copy-start.4 = (bf16[512,576]{0,1:T(8,128)(2,1)S(1)}, bf16[512,576]{0,1:T(8,128)(2,1)}, u32[]{:S(2)}) copy-start(bf16[512,576]{0,1:T(8,128)(2,1)} %param.13) | copy-start | bytes 1769476
  18.5 18.6 %copy-start.8 = (s32[16]{0:T(128)S(1)}, s32[16]{0:T(128)}, u32[]{:S(2)}) copy-start(s32[16]{0:T(128)} %param.17) | copy-start | bytes 196
  18.5 51.2 %all-to-all-start.1 = ((bf16[8,32,1536]{2,1,0:T(8,128)(2,1)}), bf16[8,32,1536]{2,1,0:T(8,128)(2,1)S(1)}, u32[]{:S(2)}, u32[]{:S(2)}) async-start(bf16[8,32,1536]{2,1,0:T(8,128)(2,1)} %stack.5), calls=%async_computation.1 | async-start | bytes 1572864 | tf_op jit(solution)/shard_map/all_to_all | solution.py:34
  31.1 183.6 %reduce-scatter.3.cloned.1.call-start = ((), (), s32[]{:S(2)}) async-start(), calls=%async_computation.4 | async-start | bytes 1179648 | tf_op jit(solution)/shard_map/reduce_scatter | solution.py:44
  31.2 6.7 %collective-permute-start = (s32[8]{0:T(128)S(1)}, s32[8]{0:T(128)S(1)}, u32[]{:S(2)}, u32[]{:S(2)}) collective-permute-start(s32[8]{0:T(128)S(1)} %copy-done.9), channel_id=1, source_target_pairs={{0,8},{8,0},{1,9},{9,1},{2,10},{10,2},{3,11},{11,3},{4,12},{12,4},... | collective-permute-start | bytes 104 | tf_op jit(solution)/shard_map/ppermute | solution.py:60
  34.6 4.8 %collective-permute-start.1 = (bf16[520,576]{1,0:T(8,128)(2,1)}, bf16[520,576]{1,0:T(8,128)(2,1)}, u32[]{:S(2)}, u32[]{:S(2)}) collective-permute-start(bf16[520,576]{1,0:T(8,128)(2,1)} %copy.50), channel_id=1, source_target_pairs={{0,8},{8,0},{1,9},{9,1},{2,10},{10,2},{3,11},{11,3},{4,12},{12,4},... | collective-permute-start | bytes 1797128 | tf_op jit(solution)/shard_map/ppermute | solution.py:60
  70.7 3.0 %copy-start.2 = (bf16[1040,576]{0,1:T(8,128)(2,1)S(1)}, bf16[1040,576]{0,1:T(8,128)(2,1)}, u32[]{:S(2)}) copy-start(bf16[1040,576]{0,1:T(8,128)(2,1)} %concatenate.30) | copy-start | bytes 3594244
  70.7 3.0 %copy-start.3 = (pred[256,1040]{0,1:T(8,128)(4,1)S(1)}, pred[256,1040]{0,1:T(8,128)(4,1)}, u32[]{:S(2)}) copy-start(pred[256,1040]{0,1:T(8,128)(4,1)} %compare_and_fusion) | copy-start | bytes 798724
  73.0 1.0 copy-start.5
  78.3 3.3 %copy-start.1 = (f32[256,8,1040]{0,2,1:T(8,128)}, f32[256,8,1040]{0,2,1:T(8,128)S(1)}, u32[]{:S(2)}) copy-start(f32[256,8,1040]{0,2,1:T(8,128)S(1)} %get-tuple-element.10) | copy-start | bytes 25559044
  151.1 88.4 %reduce-scatter.5.cloned.1.call-start = ((), (), s32[]{:S(2)}) async-start(), calls=%async_computation.5 | async-start | bytes 163840 | tf_op jit(solution)/shard_map/reduce_scatter | solution.py:44
Sparse Core Ops, SparseCore 0:
  151.2 63.4 reduce-scatter.2
  217.5 21.8 reduce-scatter.4
